TPU v7x, 256 devices: a whole 4x4x8 slice. The times are simulated.
256 devices in a mesh: dp: 8 (over y, x_hi), expert: 8 (over z), tensor: 4 (over x_lo, core).
Axes of the slice: x: 4 (x_hi: 2, x_lo: 2; x = x_hi * 2 + x_lo), y: 4, z: 8, core: 2. Of those that a mesh axis runs over, the one named last changes fastest.
Arguments:
- tokens: bfloat16 [4096, 2048], P(('dp', 'expert', 'tensor')), may hold values from -6 to 6
- cotangent: bfloat16 [4096, 2048], P(('dp', 'expert', 'tensor')), may hold values from -3 to 3
- routes: int32 [4096, 2], P(('dp', 'expert', 'tensor')), may hold values from 0 to 7, all different within a row; in each aligned block of 16 rows (0 to 15, 16 to 31, ...) at most 5 rows name the same one
- weight_codes: int32 [4096, 2], P(('dp', 'expert', 'tensor')), may hold values from 16 to 256
- dense_gate: bfloat16 [2048, 8192], P('expert', ('dp', 'tensor')), may hold values from -0.125 to 0.125
- dense_up: bfloat16 [2048, 8192], P('expert', ('dp', 'tensor')), may hold values from -0.125 to 0.125
- dense_down_t: bfloat16 [2048, 8192], P('expert', ('dp', 'tensor')), may hold values from -0.0625 to 0.0625
Outputs:
- mixed: bfloat16 [4096, 2048], P(('dp', 'expert', 'tensor'))
- input_grad: bfloat16 [4096, 2048], P(('dp', 'expert', 'tensor'))
- grad_gate: bfloat16 [8, 2048, 8192], P('expert', None, ('dp', 'tensor'))
- grad_up: bfloat16 [8, 2048, 8192], P('expert', None, ('dp', 'tensor'))
- grad_down_t: bfloat16 [8, 2048, 8192], P('expert', None, ('dp', 'tensor'))
Inputs may be any that keep to these rules, and one draw needn't show every extreme that they name: `routes`: each row names two different experts; the rows of one device name each expert at most 5 times.
All inputs are finite; a program needn't handle non-finite values.
Results may differ from a plain program's by a relative error of at most 0.02.
Values may be sent and summed in bfloat16 or wider, within the bound.
No kernel may reach another device: no remote copies, remote signals or barrier semaphores. Data moves between devices by JAX's collectives and lax.ppermute only.
A program may use at most 128 MiB of HBM per device.

v0:
```python
import jax
import jax.numpy as jnp
from jax import lax
from jax.sharding import PartitionSpec as P

GROUP = ("dp", "tensor")


def silu_parts(gate_pre):
    sigmoid_val = jax.nn.sigmoid(gate_pre)
    return (gate_pre * sigmoid_val, sigmoid_val * (1.0 + gate_pre * (1.0 - sigmoid_val)))


def contract_rows(left_side, right_side):
    return lax.dot_general(
        left_side, right_side, (((0,), (0,)), ((), ())), preferred_element_type=jnp.float32
    )


def contract_cols(left_side, right_side):
    return lax.dot_general(
        left_side, right_side, (((1,), (1,)), ((), ())), preferred_element_type=jnp.float32
    )


def forward_parts(rows_x, gate_cols, up_cols):
    gate_pre = jnp.dot(rows_x, gate_cols, preferred_element_type=jnp.float32)
    up_pre = jnp.dot(rows_x, up_cols, preferred_element_type=jnp.float32)
    activation, act_slope = silu_parts(gate_pre)
    hidden = (activation * up_pre).astype(jnp.bfloat16)
    return (up_pre, activation, act_slope, hidden)


def grad_parts(scaled, down_cols, up_pre, activation, act_slope):
    hidden_grad = jnp.dot(scaled, down_cols, preferred_element_type=jnp.float32)
    gate_grad = (hidden_grad * up_pre * act_slope).astype(jnp.bfloat16)
    up_grad = (hidden_grad * activation).astype(jnp.bfloat16)
    return (gate_grad, up_grad)


def shards(tokens, cotangent, routes, weight_codes, dense_gate, dense_up, dense_down_t):
    experts = lax.axis_size("expert")
    count_tok, model_width = tokens.shape
    hid = dense_gate.shape[1]
    capacity = 5 * count_tok // (2 * experts)
    slots_here = experts * capacity
    stacked = jnp.concatenate([dense_gate, dense_up, dense_down_t], axis=1)
    full_cols = lax.all_gather(stacked, "expert", axis=0, tiled=True)
    gate_cols = full_cols[:, :hid]
    up_cols = full_cols[:, hid : 2 * hid]
    down_cols = full_cols[:, 2 * hid :]
    gate_up_cols = full_cols[:, : 2 * hid]
    code_cols = jnp.zeros((count_tok, 128), jnp.bfloat16)
    code_cols = code_cols.at[:, 0:2].set(weight_codes.astype(jnp.bfloat16))
    home = jnp.concatenate([tokens, cotangent, code_cols], axis=1)
    plane = lax.all_gather(home, GROUP, axis=0, tiled=True)
    plane_x = plane[:, :model_width]
    plane_dy = plane[:, model_width : 2 * model_width].astype(jnp.float32)
    plane_scale = plane[:, 2 * model_width : 2 * model_width + 2].astype(jnp.float32) / 256.0
    up_pre, activation, act_slope, hidden = forward_parts(plane_x, gate_cols, up_cols)
    out_term = contract_cols(hidden, down_cols).astype(jnp.bfloat16)
    grad_term = jnp.zeros(out_term.shape, jnp.float32)
    for which in range(2):
        scaled = (plane_scale[:, which : which + 1] * plane_dy).astype(jnp.bfloat16)
        gate_grad, up_grad = grad_parts(scaled, down_cols, up_pre, activation, act_slope)
        grad_term = grad_term + contract_cols(
            jnp.concatenate([gate_grad, up_grad], axis=1), gate_up_cols
        )
    terms = jnp.concatenate([out_term, grad_term.astype(jnp.bfloat16)], axis=1)
    summed = lax.psum_scatter(terms, GROUP, scatter_dimension=0, tiled=True)
    expert_out = summed[:, :model_width].astype(jnp.float32)
    code_scale = weight_codes.astype(jnp.float32) / 256.0
    mixed = (code_scale[:, 0:1] * expert_out + code_scale[:, 1:2] * expert_out).astype(jnp.bfloat16)
    input_grad = summed[:, model_width:]
    flat_route = routes.reshape(-1)
    flat_scale = weight_codes.reshape(-1).astype(jnp.float32) / 256.0
    onehot = (flat_route[:, None] == jnp.arange(experts, dtype=jnp.int32)[None, :]).astype(
        jnp.int32
    )
    earlier = jnp.cumsum(onehot, axis=0) - onehot
    slot_of = flat_route * capacity + jnp.sum(earlier * onehot, axis=1)
    placed = (slot_of[None, :] == jnp.arange(slots_here, dtype=jnp.int32)[:, None]).astype(
        jnp.bfloat16
    )
    flat_x = jnp.repeat(tokens, 2, axis=0)
    flat_scaled = (
        flat_scale[:, None] * jnp.repeat(cotangent, 2, axis=0).astype(jnp.float32)
    ).astype(jnp.bfloat16)
    send_x = jnp.dot(placed, flat_x, preferred_element_type=jnp.float32).astype(jnp.bfloat16)
    send_s = jnp.dot(placed, flat_scaled, preferred_element_type=jnp.float32).astype(jnp.bfloat16)
    send = jnp.stack(
        [
            send_x.reshape(experts, capacity, model_width),
            send_s.reshape(experts, capacity, model_width),
        ],
        axis=1,
    )
    got = lax.all_to_all(send, "expert", split_axis=0, concat_axis=0, tiled=True)
    got = jnp.transpose(got, (1, 0, 2, 3))
    rows = lax.all_gather(got, GROUP, axis=1, tiled=True)
    rows_x = rows[0].reshape(-1, model_width)
    rows_s = rows[1].reshape(-1, model_width)
    r_up, r_act, r_slope, r_hidden = forward_parts(rows_x, gate_cols, up_cols)
    r_gate, r_upg = grad_parts(rows_s, down_cols, r_up, r_act, r_slope)
    grad_gate = contract_rows(rows_x, r_gate).astype(jnp.bfloat16)[None]
    grad_up = contract_rows(rows_x, r_upg).astype(jnp.bfloat16)[None]
    grad_down_t = contract_rows(rows_s, r_hidden).astype(jnp.bfloat16)[None]
    return (mixed, input_grad, grad_gate, grad_up, grad_down_t)


def solution(mesh):
    rows = P(("dp", "expert", "tensor"), None)
    weights = P("expert", ("dp", "tensor"))
    grads = P("expert", None, ("dp", "tensor"))
    return jax.shard_map(
        shards,
        mesh=mesh,
        in_specs=(rows, rows, rows, rows, weights, weights, weights),
        out_specs=(rows, rows, grads, grads, grads),
        check_vma=False,
    )
```

profile of v0, /device:TPU:1, one launch (start us, length us, event | category | flops | bytes accessed | tf_op | source)
XLA Modules:
  0.0 376.8 jit_solution(17290189949668021922)
XLA Ops:
  7.2 0.6 compare_reduce_fusion
  7.9 1.3 broadcast_select_fusion
  9.2 0.1 copy.28
  9.3 1.5 fusion.43
  10.9 1.8 pad_maximum_fusion.2
  12.8 54.0 %all-gather.4.cloned.1.call-done = bf16[512,4224]{1,0:T(8,128)(2,1)} async-done(((bf16[16,4224]{1,0:T(8,128)(2,1)}), bf16[512,4224]{1,0:T(8,128)(2,1)}) %all-gather.4.cloned.1.call-update) | async-done | bytes 4325392 | tf_op jit(solution)/shard_map/all_gather | solution.py:56
  66.7 0.9 convert_multiply_fusion.2
  67.7 0.3 slice_reduce_fusion.2
  68.0 44.9 %all-gather.6.cloned.1.call-done = bf16[2048,768]{1,0:T(8,128)(2,1)} async-done(((bf16[256,768]{1,0:T(8,128)(2,1)}), bf16[2048,768]{1,0:T(8,128)(2,1)}) %all-gather.6.cloned.1.call-update) | async-done | bytes 3145744 | tf_op jit(solution)/shard_map/all_gather | solution.py:48
  112.9 2.8 fusion.16
  115.7 0.1 copy-done.1
  115.8 2.5 fusion.18
  118.3 0.4 copy-done.5
  118.6 0.8 fusion.7
  119.5 0.8 convolution_convert_fusion
  120.3 1.0 multiply_convert_fusion.7
  121.3 1.3 fusion.12
  122.6 1.3 add_convert_fusion
  123.9 2.6 pad_maximum_fusion
  126.6 0.6 copy-done.6
  127.3 0.1 reshape.63
  127.4 0.1 copy.24
  127.5 0.1 div.27
  127.6 0.1 broadcast_in_dim.21
  127.7 0.9 convert_element_type.107
  128.7 0.2 select_reduce_fusion
  128.9 1.9 convolution_convert_fusion.4
  130.7 1.0 stack_reshape.7
  131.7 0.7 broadcast_in_dim.20
  132.5 1.0 reshape.64
  133.4 0.8 convolution_convert_fusion.5
  134.3 1.7 stack_reshape.6
  136.0 1.1 pad_maximum_fusion.1
  137.0 0.4 copy.25
  137.4 15.5 %all_to_all.5 = bf16[8,2,5,2048]{3,1,2,0:T(2,128)(2,1)} all-to-all(bf16[8,2,5,2048]{3,1,2,0:T(2,128)(2,1)S(1)} %copy.25), channel_id=1, replica_groups=mesh['dp'=8,'expert'=8,'tensor'=4] {'expert'}, dimensions={0} | all-to-all | bytes 655360 | tf_op jit(solution)/shard_map/all_to_all | solution.py:98
  152.9 60.5 %reduce-scatter.2.cloned.1.call-done = bf16[16,4096]{1,0:T(8,128)(2,1)} async-done(((bf16[512,4096]{1,0:T(8,128)(2,1)}), bf16[16,4096]{1,0:T(8,128)(2,1)}) %reduce-scatter.2.cloned.1.call-update) | async-done | bytes 131088 | tf_op jit(solution)/shard_map/reduce_scatter | solution.py:70
  213.4 1.5 slice.86
  214.9 1.5 multiply_convert_fusion.14
  216.5 64.0 %all-gather.8.cloned.1.call-done = bf16[2,256,5,2048]{3,0,2,1:T(2,128)(2,1)} async-done(((bf16[2,8,5,2048]{3,0,2,1:T(2,128)(2,1)}), bf16[2,256,5,2048]{3,0,2,1:T(2,128)(2,1)}) %all-gather.8.cloned.1.call-update) | async-done | bytes 10485776 | tf_op jit(solution)/shard_map/all_gather | solution.py:100
  280.5 53.6 %slice_reduce_fusion = (bf16[256,5,2048]{2,1,0:T(8,128)(2,1)}, bf16[256,5,2048]{2,1,0:T(8,128)(2,1)}) fusion(bf16[2,256,5,2048]{3,0,2,1:T(2,128)(2,1)} %all-gather.8.cloned.1.call-done), kind=kLoop, calls=%fused_computation | loop fusion | bytes 20971520 | tf_op jit(solution)/shard_map/slice | solution.py:102
  334.1 10.0 %reshape_squeeze.6 = bf16[1280,2048]{1,0:T(8,128)(2,1)} reshape(bf16[256,5,2048]{2,1,0:T(8,128)(2,1)} %get-tuple-element.18) | data formatting | bytes 10485760 | tf_op jit(solution)/shard_map/reshape;squeeze | solution.py:101
  344.2 10.0 %reshape_squeeze.7 = bf16[1280,2048]{1,0:T(8,128)(2,1)} reshape(bf16[256,5,2048]{2,1,0:T(8,128)(2,1)} %get-tuple-element.17) | data formatting | bytes 10485760 | tf_op jit(solution)/shard_map/reshape;squeeze | solution.py:102
  354.2 4.2 %fusion.24 = f32[1280,256]{1,0:T(8,128)S(1)} fusion(bf16[1280,2048]{1,0:T(8,128)(2,1)} %reshape_squeeze.6, bf16[2048,768]{1,0:T(8,128)(2,1)S(1)} %copy-done.1), kind=kOutput, calls=%fused_computation.38 | convolution fusion | flops 1342177280 | bytes 7602176 | tf_op jit(solution)/shard_map/dot_general | solution.py:27
  358.4 1.6 fusion.21
  360.0 2.9 fusion.4
  362.8 1.6 fusion.27
  364.4 2.9 fusion.3
  367.3 3.0 fusion.2
  (30 shorter events, 0.5 us)
Async XLA Ops:
  7.2 59.6 %all-gather.4.cloned.1.call-start = ((), (), s32[]{:S(2)}) async-start(), calls=%async_computation.2 | async-start | bytes 4460544 | tf_op jit(solution)/shard_map/all_gather | solution.py:56
  10.8 102.1 %all-gather.6.cloned.1.call-start = ((), (), s32[]{:S(2)}) async-start(), calls=%async_computation.3 | async-start | bytes 3538944 | tf_op jit(solution)/shard_map/all_gather | solution.py:48
  12.7 200.7 %reduce-scatter.2.cloned.1.call-start = ((), (), s32[]{:S(2)}) async-start(), calls=%async_computation.4 | async-start | bytes 4325376 | tf_op jit(solution)/shard_map/reduce_scatter | solution.py:70
  112.9 2.9 copy-start.1
  115.8 2.9 copy-start.5
  126.5 0.7 copy-start.6
  126.5 0.9 copy-start.4
  126.5 1.0 copy-start.2
  126.5 5.2 %copy-start.3 = (bf16[16,2048]{1,0:T(8,128)(2,1)S(1)}, bf16[16,2048]{1,0:T(8,128)(2,1)}, u32[]{:S(2)}) copy-start(bf16[16,2048]{1,0:T(8,128)(2,1)} %param.9) | copy-start | bytes 196612
  126.5 154.0 %all-gather.8.cloned.1.call-start = ((), (), s32[]{:S(2)}) async-start(), calls=%async_computation.5 | async-start | bytes 10813440 | tf_op jit(solution)/shard_map/all_gather | solution.py:100
  354.2 4.2 %copy-start = (bf16[1280,2048]{1,0:T(8,128)(2,1)S(1)}, bf16[1280,2048]{1,0:T(8,128)(2,1)}, u32[]{:S(2)}) copy-start(bf16[1280,2048]{1,0:T(8,128)(2,1)} %reshape_squeeze.6) | copy-start | bytes 15728644
  354.2 5.8 %slice-start = ((s8[5242880]{0:T(1024)(128)(4,1)}), s8[4194304]{0:T(1024)(128)(4,1)S(1)}, s32[]{:S(2)}) async-start(s8[5242880]{0:T(1024)(128)(4,1)} %bitcast.16), calls=%async_computation.6 | async-start | bytes 8388608
  358.4 1.6 slice-start.1
Sparse Core Ops, SparseCore 0:
  11.2 55.5 all-gather.3
  69.1 43.7 all-gather.5
  126.7 86.7 reduce-scatter.1
  216.2 64.2 all-gather.7
where the time goes:
time: 378 us; the launch traced here: 377 us
  waiting for transfers between devices  224 us (59%)
  local copies, waits for them, and re-layouts  82.6 us (22%)
  matrix products  29.2 us (8%)
  blocking collectives  15.5 us (4%)
  between operations  14 us (4%)
  other arithmetic  11.7 us (3%)
    all_gather x1, waiting for transfers between devices, shards(): rows = lax.all_gather(got, GROUP, axis=1, tiled=True)  64 us
    reduce_scatter x1, waiting for transfers between devices, shards(): summed = lax.psum_scatter(terms, GROUP, scatter_dimension=0, tiled=True)  60.5 us
    all_gather x1, waiting for transfers between devices, shards(): plane = lax.all_gather(home, GROUP, axis=0, tiled=True)  54 us
    slice x1, local copies, waits for them, and re-layouts, shards(): rows_s = rows[1].reshape(-1, model_width)  53.6 us
    all_gather x1, waiting for transfers between devices, shards(): full_cols = lax.all_gather(stacked, 'expert', axis=0, tiled=True)  44.9 us
    all_to_all x1, blocking collectives, shards(): lax.all_to_all(send, 'expert', split_axis=0, concat_axis=0, tiled=True)  15.5 us
    another operation x1, local copies, waits for them, and re-layouts, shards(): rows_x = rows[0].reshape(-1, model_width)  10 us
    another operation x1, local copies, waits for them, and re-layouts, shards(): rows_s = rows[1].reshape(-1, model_width)  10 us
  transfers between devices with their start and end apart: 4, of which 4 were waited for; matrix products, arithmetic and copies ran while one was open for 4% of the time, Pallas kernels for 0%

commit v1 on v0

--- a/solution.py
+++ b/solution.py
@@ -45,7 +45,24 @@
     capacity = 5 * count_tok // (2 * experts)
     slots_here = experts * capacity
     stacked = jnp.concatenate([dense_gate, dense_up, dense_down_t], axis=1)
-    full_cols = lax.all_gather(stacked, "expert", axis=0, tiled=True)
+    ways, here, step = (lax.axis_size("expert"), lax.axis_index("expert"), stacked.shape[0])
+    lengths = [n * ways if d == 0 else n for d, n in enumerate(stacked.shape)]
+    full_cols = lax.dynamic_update_slice_in_dim(
+        jnp.zeros(lengths, stacked.dtype), stacked, here * step, axis=0
+    )
+    going_up = going_down = stacked
+    for far in range(1, ways // 2 + 1):
+        going_up = lax.ppermute(going_up, "expert", [(d, (d + 1) % ways) for d in range(ways)])
+        full_cols = lax.dynamic_update_slice_in_dim(
+            full_cols, going_up, (here - far) % ways * step, axis=0
+        )
+        if 2 * far < ways:
+            going_down = lax.ppermute(
+                going_down, "expert", [(d, (d - 1) % ways) for d in range(ways)]
+            )
+            full_cols = lax.dynamic_update_slice_in_dim(
+                full_cols, going_down, (here + far) % ways * step, axis=0
+            )
     gate_cols = full_cols[:, :hid]
     up_cols = full_cols[:, hid : 2 * hid]
     down_cols = full_cols[:, 2 * hid :]

time: 378 us -> 338 us (0.89)
  waiting for transfers between devices: 224 us -> 154 us
  starting transfers between devices: 0.16 us -> 11.4 us
  local copies, waits for them, and re-layouts: 82.6 us -> 91.9 us
  matrix products: 29.2 us -> 34.4 us
  blocking collectives: 15.5 us -> 19.4 us
    all_gather x1, waiting for transfers between devices: 54 us -> 8.1 us  [shards(): plane = lax.all_gather(home, GROUP, axis=0, tiled=True)]
    all_gather x1 -> x0, waiting for transfers between devices: 44.9 us -> none  [shards(): full_cols = lax.all_gather(stacked, 'expert', axis=0, tiled=True)]
    ppermute x0 -> x7, waiting for transfers between devices: none -> 27.7 us  [the longest x4 27.7 us: shards(): lax.ppermute(going_up, 'expert', [(d, (d + 1) % ways) for d in range(ways)])]
    ppermute x0 -> x7, starting transfers between devices: none -> 11.3 us  [the longest x3 8.72 us: shards(): lax.ppermute(going_down, 'expert', [(d, (d - 1) % ways) for d in range(wa...]
    reduce_scatter x1, waiting for transfers between devices: 60.5 us -> 54.4 us  [shards(): summed = lax.psum_scatter(terms, GROUP, scatter_dimension=0, tiled=True)]
    dynamic_update_slice x0 -> x8, local copies, waits for them, and re-layouts: none -> 4.29 us  [the longest x4 2.17 us: shards(): lax.dynamic_update_slice_in_dim(full_cols, going_up, (here - far) % ways...]
    all_to_all x1, blocking collectives: 15.5 us -> 19.4 us  [shards(): lax.all_to_all(send, 'expert', split_axis=0, concat_axis=0, tiled=True)]
  transfers between devices with their start and end apart: 4 -> 10, of which waited for: 4 -> 7; matrix products, arithmetic and copies ran while one was open for 4% -> 7% of each run, Pallas kernels for 0% -> 0%
where the time goes in v1:
time: 338 us; the launch traced here: 337 us
  waiting for transfers between devices  154 us (46%)
  local copies, waits for them, and re-layouts  91.9 us (27%)
  matrix products  34.4 us (10%)
  blocking collectives  19.4 us (6%)
  between operations  14 us (4%)
  starting transfers between devices  11.4 us (3%)
  other arithmetic  11.4 us (3%)
    all_gather x1, waiting for transfers between devices, shards(): rows = lax.all_gather(got, GROUP, axis=1, tiled=True)  64.2 us
    reduce_scatter x1, waiting for transfers between devices, shards(): summed = lax.psum_scatter(terms, GROUP, scatter_dimension=0, tiled=True)  54.4 us
    slice x1, local copies, waits for them, and re-layouts, shards(): rows_s = rows[1].reshape(-1, model_width)  53.6 us
    ppermute x4, waiting for transfers between devices, shards(): lax.ppermute(going_up, 'expert', [(d, (d + 1) % ways) for d in range(ways)])  27.7 us
    all_to_all x1, blocking collectives, shards(): lax.all_to_all(send, 'expert', split_axis=0, concat_axis=0, tiled=True)  19.4 us
    dot_general x3, matrix products, contract_rows(): lax.dot_general(left_side, right_side, (((0,), (0,)), ((), ())), preferre...  11.2 us
    another operation x1, local copies, waits for them, and re-layouts, shards(): rows_s = rows[1].reshape(-1, model_width)  10 us
    another operation x1, local copies, waits for them, and re-layouts, shards(): rows_x = rows[0].reshape(-1, model_width)  10 us
  transfers between devices with their start and end apart: 10, of which 7 were waited for; matrix products, arithmetic and copies ran while one was open for 7% of the time, Pallas kernels for 0%

profile of v1, /device:TPU:1, one launch (start us, length us, event | category | flops | bytes accessed | tf_op | source)
XLA Modules:
  0.0 337.0 jit_solution(12024688188019249340)
XLA Ops:
  7.9 1.3 broadcast_select_fusion
  9.3 1.5 fusion.43
  10.9 0.9 constant_dynamic-update-slice_fusion.2
  11.8 0.9 constant_dynamic-update-slice_fusion.1
  12.7 0.9 constant_dynamic-update-slice_fusion
  13.6 2.5 collective-permute-start
  16.2 4.0 %collective-permute-start.1 = (bf16[256,768]{1,0:T(8,128)(2,1)S(1)}, bf16[256,768]{1,0:T(8,128)(2,1)}, u32[]{:S(2)}, u32[]{:S(2)}) collective-permute-start(bf16[256,768]{1,0:T(8,128)(2,1)S(1)} %constant_dynamic-update-slice_fusion), channel_id=1, source_target_pairs={{0,28},{4,0},{8,4},{12,8},{16,12},{20,16},{24,20},{28,24},{1,29},{... | collective-permute-start | bytes 1179656 | tf_op jit(solution)/shard_map/ppermute | solution.py:60
  20.2 8.8 %collective-permute-done = bf16[256,768]{1,0:T(8,128)(2,1)S(1)} collective-permute-done((bf16[256,768]{1,0:T(8,128)(2,1)S(1)}, bf16[256,768]{1,0:T(8,128)(2,1)S(1)}, u32[]{:S(2)}, u32[]{:S(2)}) %collective-permute-start) | collective-permute-done | bytes 393248 | tf_op jit(solution)/shard_map/ppermute | solution.py:55
  29.7 1.9 collective-permute-start.3
  31.7 8.0 %collective-permute-done.2 = bf16[256,768]{1,0:T(8,128)(2,1)} collective-permute-done((bf16[256,768]{1,0:T(8,128)(2,1)S(1)}, bf16[256,768]{1,0:T(8,128)(2,1)}, u32[]{:S(2)}, u32[]{:S(2)}) %collective-permute-start.2) | collective-permute-done | bytes 393248 | tf_op jit(solution)/shard_map/ppermute | solution.py:55
  40.7 2.7 collective-permute-start.5
  43.5 1.0 constant_dynamic-update-slice_fusion.8
  44.5 5.2 %collective-permute-done.4 = bf16[256,768]{1,0:T(8,128)(2,1)} collective-permute-done((bf16[256,768]{1,0:T(8,128)(2,1)}, bf16[256,768]{1,0:T(8,128)(2,1)}, u32[]{:S(2)}, u32[]{:S(2)}) %collective-permute-start.4) | collective-permute-done | bytes 393248 | tf_op jit(solution)/shard_map/ppermute | solution.py:55
  49.7 1.1 constant_dynamic-update-slice_fusion.7
  50.7 1.0 constant_dynamic-update-slice_fusion.6
  51.8 1.0 constant_dynamic-update-slice_fusion.5
  52.9 5.8 %collective-permute-done.6 = bf16[256,768]{1,0:T(8,128)(2,1)S(1)} collective-permute-done((bf16[256,768]{1,0:T(8,128)(2,1)}, bf16[256,768]{1,0:T(8,128)(2,1)S(1)}, u32[]{:S(2)}, u32[]{:S(2)}) %collective-permute-start.6) | collective-permute-done | bytes 393248 | tf_op jit(solution)/shard_map/ppermute | solution.py:55
  58.6 8.1 %all-gather.3.cloned.1.call-done = bf16[512,4224]{1,0:T(8,128)(2,1)} async-done(((bf16[16,4224]{1,0:T(8,128)(2,1)}), bf16[512,4224]{1,0:T(8,128)(2,1)}) %all-gather.3.cloned.1.call-update) | async-done | bytes 4325392 | tf_op jit(solution)/shard_map/all_gather | solution.py:73
  66.7 1.1 convert_multiply_fusion.2
  68.1 2.3 fusion.16
  71.2 0.8 convolution_convert_fusion
  72.0 0.9 fusion.5
  72.9 1.1 multiply_convert_fusion.9
  74.0 1.3 fusion.11
  75.3 1.3 add_convert_fusion
  76.6 2.5 pad_maximum_fusion
  81.4 0.9 convert_element_type.107
  82.3 0.8 select_reduce_fusion
  83.8 1.9 convolution_convert_fusion.4
  85.7 1.0 stack_reshape.7
  87.4 1.0 reshape.64
  88.4 0.8 convolution_convert_fusion.5
  89.2 1.7 stack_reshape.6
  90.9 1.1 pad_maximum_fusion.1
  92.4 19.4 %all_to_all.5 = bf16[8,2,5,2048]{3,1,2,0:T(2,128)(2,1)} all-to-all(bf16[8,2,5,2048]{3,1,2,0:T(2,128)(2,1)S(1)} %copy.25), channel_id=1, replica_groups=mesh['dp'=8,'expert'=8,'tensor'=4] {'expert'}, dimensions={0} | all-to-all | bytes 655360 | tf_op jit(solution)/shard_map/all_to_all | solution.py:115
  111.8 54.4 %reduce-scatter.2.cloned.1.call-done = bf16[16,4096]{1,0:T(8,128)(2,1)} async-done(((bf16[512,4096]{1,0:T(8,128)(2,1)}), bf16[16,4096]{1,0:T(8,128)(2,1)}) %reduce-scatter.2.cloned.1.call-update) | async-done | bytes 131088 | tf_op jit(solution)/shard_map/reduce_scatter | solution.py:87
  166.2 1.5 slice.86
  167.7 1.5 multiply_convert_fusion.14
  169.3 64.2 %all-gather.5.cloned.1.call-done = bf16[2,256,5,2048]{3,0,2,1:T(2,128)(2,1)} async-done(((bf16[2,8,5,2048]{3,0,2,1:T(2,128)(2,1)}), bf16[2,256,5,2048]{3,0,2,1:T(2,128)(2,1)}) %all-gather.5.cloned.1.call-update) | async-done | bytes 10485776 | tf_op jit(solution)/shard_map/all_gather | solution.py:117
  233.5 53.6 %slice_reduce_fusion = (bf16[256,5,2048]{2,1,0:T(8,128)(2,1)}, bf16[256,5,2048]{2,1,0:T(8,128)(2,1)}) fusion(bf16[2,256,5,2048]{3,0,2,1:T(2,128)(2,1)} %all-gather.5.cloned.1.call-done), kind=kLoop, calls=%fused_computation | loop fusion | bytes 20971520 | tf_op jit(solution)/shard_map/slice | solution.py:119
  287.1 10.0 %reshape_squeeze.6 = bf16[1280,2048]{1,0:T(8,128)(2,1)} reshape(bf16[256,5,2048]{2,1,0:T(8,128)(2,1)} %get-tuple-element.18) | data formatting | bytes 10485760 | tf_op jit(solution)/shard_map/reshape;squeeze | solution.py:118
  297.1 5.2 %fusion.21 = f32[1280,256]{1,0:T(8,128)} fusion(bf16[1280,2048]{1,0:T(8,128)(2,1)} %reshape_squeeze.6, bf16[2048,768]{1,0:T(8,128)(2,1)S(1)} %constant_dynamic-update-slice_fusion.3), kind=kOutput, calls=%fused_computation.35 | convolution fusion | flops 1342177280 | bytes 7602176 | tf_op jit(solution)/shard_map/dot_general | solution.py:28
  302.3 2.6 fusion.24
  304.9 10.0 %reshape_squeeze.7 = bf16[1280,2048]{1,0:T(8,128)(2,1)} reshape(bf16[256,5,2048]{2,1,0:T(8,128)(2,1)} %get-tuple-element.17) | data formatting | bytes 10485760 | tf_op jit(solution)/shard_map/reshape;squeeze | solution.py:119
  315.0 4.2 %fusion.27 = f32[1280,256]{1,0:T(8,128)S(1)} fusion(bf16[1280,2048]{1,0:T(8,128)(2,1)} %reshape_squeeze.7, bf16[2048,768]{1,0:T(8,128)(2,1)S(1)} %constant_dynamic-update-slice_fusion.3), kind=kOutput, calls=%fused_computation.41 | convolution fusion | flops 1342177280 | bytes 7602176 | tf_op jit(solution)/shard_map/dot_general | solution.py:35
  319.2 5.4 %fusion.4 = bf16[1,2048,256]{2,1,0:T(8,128)(2,1)} fusion(bf16[1280,2048]{1,0:T(8,128)(2,1)} %reshape_squeeze.7, f32[1280,256]{1,0:T(8,128)S(1)} %copy-done.11, f32[1280,256]{1,0:T(8,128)S(1)} %copy-done.12), kind=kOutput, calls=%fused_computation.14 | convolution fusion | flops 1344667648 | bytes 8912896 | tf_op jit(solution)/shard_map/dot_general | solution.py:15
  324.6 2.9 fusion.3
  327.5 3.0 fusion.2
  (64 shorter events, 7.8 us)
Async XLA Ops:
  7.2 59.6 %all-gather.3.cloned.1.call-start = ((), (), s32[]{:S(2)}) async-start(), calls=%async_computation.2 | async-start | bytes 4460544 | tf_op jit(solution)/shard_map/all_gather | solution.py:73
  10.8 155.4 %reduce-scatter.2.cloned.1.call-start = ((), (), s32[]{:S(2)}) async-start(), calls=%async_computation.3 | async-start | bytes 4325376 | tf_op jit(solution)/shard_map/reduce_scatter | solution.py:87
  13.6 15.3 %collective-permute-start = (bf16[256,768]{1,0:T(8,128)(2,1)S(1)}, bf16[256,768]{1,0:T(8,128)(2,1)S(1)}, u32[]{:S(2)}, u32[]{:S(2)}) collective-permute-start(bf16[256,768]{1,0:T(8,128)(2,1)S(1)} %constant_dynamic-update-slice_fusion), channel_id=1, source_target_pairs={{0,4},{4,8},{8,12},{12,16},{16,20},{20,24},{24,28},{28,0},{1,5},{5... | collective-permute-start | bytes 1179656 | tf_op jit(solution)/shard_map/ppermute | solution.py:55
  16.2 12.8 %collective-permute-start.1 = (bf16[256,768]{1,0:T(8,128)(2,1)S(1)}, bf16[256,768]{1,0:T(8,128)(2,1)}, u32[]{:S(2)}, u32[]{:S(2)}) collective-permute-start(bf16[256,768]{1,0:T(8,128)(2,1)S(1)} %constant_dynamic-update-slice_fusion), channel_id=1, source_target_pairs={{0,28},{4,0},{8,4},{12,8},{16,12},{20,16},{24,20},{28,24},{1,29},{... | collective-permute-start | bytes 1179656 | tf_op jit(solution)/shard_map/ppermute | solution.py:60
  29.0 0.7 copy-start.1
  29.0 10.7 %collective-permute-start.2 = (bf16[256,768]{1,0:T(8,128)(2,1)S(1)}, bf16[256,768]{1,0:T(8,128)(2,1)}, u32[]{:S(2)}, u32[]{:S(2)}) collective-permute-start(bf16[256,768]{1,0:T(8,128)(2,1)S(1)} %collective-permute-done), channel_id=1, source_target_pairs={{0,4},{4,8},{8,12},{12,16},{16,20},{20,24},{24,28},{28,0},{1,5},{5... | collective-permute-start | bytes 1179656 | tf_op jit(solution)/shard_map/ppermute | solution.py:55
  29.7 11.0 %collective-permute-start.3 = (bf16[256,768]{1,0:T(8,128)(2,1)}, bf16[256,768]{1,0:T(8,128)(2,1)}, u32[]{:S(2)}, u32[]{:S(2)}) collective-permute-start(bf16[256,768]{1,0:T(8,128)(2,1)} %collective-permute-done.1), channel_id=1, source_target_pairs={{0,28},{4,0},{8,4},{12,8},{16,12},{20,16},{24,20},{28,24},{1,29},{... | collective-permute-start | bytes 1179656 | tf_op jit(solution)/shard_map/ppermute | solution.py:60
  39.7 10.0 %collective-permute-start.4 = (bf16[256,768]{1,0:T(8,128)(2,1)}, bf16[256,768]{1,0:T(8,128)(2,1)}, u32[]{:S(2)}, u32[]{:S(2)}) collective-permute-start(bf16[256,768]{1,0:T(8,128)(2,1)} %collective-permute-done.2), channel_id=1, source_target_pairs={{0,4},{4,8},{8,12},{12,16},{16,20},{20,24},{24,28},{28,0},{1,5},{5... | collective-permute-start | bytes 1179656 | tf_op jit(solution)/shard_map/ppermute | solution.py:55
  39.7 1.0 copy-start.2
  40.7 12.1 %collective-permute-start.5 = (bf16[256,768]{1,0:T(8,128)(2,1)}, bf16[256,768]{1,0:T(8,128)(2,1)S(1)}, u32[]{:S(2)}, u32[]{:S(2)}) collective-permute-start(bf16[256,768]{1,0:T(8,128)(2,1)} %collective-permute-done.3), channel_id=1, source_target_pairs={{0,28},{4,0},{8,4},{12,8},{16,12},{20,16},{24,20},{28,24},{1,29},{... | collective-permute-start | bytes 1179656 | tf_op jit(solution)/shard_map/ppermute | solution.py:60
  49.7 9.0 %collective-permute-start.6 = (bf16[256,768]{1,0:T(8,128)(2,1)}, bf16[256,768]{1,0:T(8,128)(2,1)S(1)}, u32[]{:S(2)}, u32[]{:S(2)}) collective-permute-start(bf16[256,768]{1,0:T(8,128)(2,1)} %collective-permute-done.4), channel_id=1, source_target_pairs={{0,4},{4,8},{8,12},{12,16},{16,20},{20,24},{24,28},{28,0},{1,5},{5... | collective-permute-start | bytes 1179656 | tf_op jit(solution)/shard_map/ppermute | solution.py:55
  66.7 3.7 %copy-start.9 = (bf16[512,4224]{1,0:T(8,128)(2,1)S(1)}, bf16[512,4224]{1,0:T(8,128)(2,1)}, u32[]{:S(2)}) copy-start(bf16[512,4224]{1,0:T(8,128)(2,1)} %all-gather.3.cloned.1.call-done) | copy-start | bytes 12976132
  79.1 0.7 copy-start.10
  79.1 1.0 copy-start.8
  79.1 2.2 copy-start.3
  79.2 7.5 %copy-start.4 = (bf16[16,2048]{1,0:T(8,128)(2,1)S(1)}, bf16[16,2048]{1,0:T(8,128)(2,1)}, u32[]{:S(2)}) copy-start(bf16[16,2048]{1,0:T(8,128)(2,1)} %param.9) | copy-start | bytes 196612
  79.2 154.3 %all-gather.5.cloned.1.call-start = ((), (), s32[]{:S(2)}) async-start(), calls=%async_computation.4 | async-start | bytes 10813440 | tf_op jit(solution)/shard_map/all_gather | solution.py:117
  80.0 0.5 copy-start.5
  80.1 0.6 copy-start.6
  83.1 28.7 %copy-start.7 = (f32[16,2]{0,1:T(2,128)S(1)}, f32[16,2]{0,1:T(2,128)}, u32[]{:S(2)}) copy-start(f32[16,2]{0,1:T(2,128)} %copy-done.6) | copy-start | bytes 388
  297.1 5.2 %copy-start = (bf16[1280,2048]{1,0:T(8,128)(2,1)S(1)}, bf16[1280,2048]{1,0:T(8,128)(2,1)}, u32[]{:S(2)}) copy-start(bf16[1280,2048]{1,0:T(8,128)(2,1)} %reshape_squeeze.6) | copy-start | bytes 15728644
  315.0 4.2 %copy-start.11 = (f32[1280,256]{1,0:T(8,128)S(1)}, f32[1280,256]{1,0:T(8,128)}, u32[]{:S(2)}) copy-start(f32[1280,256]{1,0:T(8,128)} %fusion.21) | copy-start | bytes 3932164
  315.0 4.2 %copy-start.12 = (f32[1280,256]{1,0:T(8,128)S(1)}, f32[1280,256]{1,0:T(8,128)}, u32[]{:S(2)}) copy-start(f32[1280,256]{1,0:T(8,128)} %fusion.24) | copy-start | bytes 3932164
  315.0 9.6 %slice-start = ((s8[5242880]{0:T(1024)(128)(4,1)}), s8[4194304]{0:T(1024)(128)(4,1)S(1)}, s32[]{:S(2)}) async-start(s8[5242880]{0:T(1024)(128)(4,1)} %bitcast.16), calls=%async_computation.5 | async-start | bytes 8388608
  319.2 5.4 %slice-start.1 = ((s8[5242880]{0:T(1024)(128)(4,1)}), s8[1048576]{0:T(1024)(128)(4,1)S(1)}, s32[]{:S(2)}) async-start(s8[5242880]{0:T(1024)(128)(4,1)} %bitcast.16), calls=%async_computation.6 | async-start | bytes 2097152
Sparse Core Ops, SparseCore 0:
  11.2 55.5 all-gather.2
  79.3 86.8 reduce-scatter.1
  169.1 64.3 all-gather.4
